TPU v7x, 256 devices: a whole 4x4x8 slice. The times are simulated.
256 devices in a mesh: band: 16 (over x, y_lo, core), dom: 16 (over z, y_hi).
Axes of the slice: x: 4, y: 4 (y_hi: 2, y_lo: 2; y = y_hi * 2 + y_lo), z: 8, core: 2. Of those that a mesh axis runs over, the one named last changes fastest.
Arguments:
- psi: float32 [1024, 64, 8, 128], P('band', 'dom'), may hold values from -6 to 6
- potential: float32 [64, 8, 128], P('dom'), may hold values from -1 to 1
- owner: int32 [1], replicated, may hold values from 0 to 15
Outputs:
- filtered: float32 [1024, 64, 8, 128], P('band', 'dom')
- intersection: float32 [64, 1024], P(None, 'band')
- hamiltonian: float32 [64, 1024], P(None, 'band')
Inputs may be any that keep to these rules, and one draw needn't show every extreme that they name: The owner's panel holds bands 64 * owner to 64 * owner + 63.
All inputs are finite; a program needn't handle non-finite values.
Results may differ from a plain program's by a relative error of at most 0.000084.
Values sent between devices are 32-bit elements; how exact they have to be, the bound alone decides.
No kernel may reach another device: no remote copies, remote signals or barrier semaphores. Data moves between devices by JAX's collectives and lax.ppermute only.
A program may use at most 64 MiB of HBM per device.

v0:
```python
import jax
import jax.numpy as jnp
from jax import lax
from jax.sharding import PartitionSpec as P

center = 4.9
halfwidth = 4.1


def extended_2(block, sides, width):
    for axis, dim in sides:
        count = lax.axis_size(axis)
        forward = [(i, i + 1) for i in range(count - 1)]
        forward.append((count - 1, 0))
        backward = [(target, source) for source, target in forward]
        low = lax.ppermute(
            lax.slice_in_dim(block, block.shape[dim] - width, None, axis=dim), axis, forward
        )
        high = lax.ppermute(lax.slice_in_dim(block, 0, width, axis=dim), axis, backward)
        block = jnp.concatenate([low, block, high], axis=dim)
    return block


def broadcast(array, axis, root):
    mine = lax.axis_index(axis) == root
    return lax.psum(jnp.where(mine, array, jnp.zeros_like(array)), axis)


def lap_periodic(grid_field, which_axis):
    outer = jnp.roll(grid_field, 2, which_axis) + jnp.roll(grid_field, -2, which_axis)
    nearer = jnp.roll(grid_field, 1, which_axis) + jnp.roll(grid_field, -1, which_axis)
    return -1.0 / 12.0 * outer + 4.0 / 3.0 * nearer - 2.5 * grid_field


def hamiltonian_apply(extended, local_potential):
    interior = extended[:, 2:-2]
    along_first = (
        -1.0 / 12.0 * (extended[:, :-4] + extended[:, 4:])
        + 4.0 / 3.0 * (extended[:, 1:-3] + extended[:, 3:-1])
        - 2.5 * interior
    )
    laplace = along_first + lap_periodic(interior, 2) + lap_periodic(interior, 3)
    return -0.5 * laplace + local_potential * interior


def shifted(extended, local_potential):
    return (hamiltonian_apply(extended, local_potential) - center * extended[:, 2:-2]) / halfwidth


def with_faces(grid_field):
    return extended_2(grid_field, (("dom", 1),), 2)


def body(psi, potential, owner):
    current = psi
    first_term = shifted(with_faces(current), potential)
    current = 2.0 * shifted(with_faces(first_term), potential) - current
    local_bands = current.shape[0]
    owner_root = owner[0]
    owned_panel = broadcast(current, "band", owner_root)
    total_cells = current.shape[1] * current.shape[2] * current.shape[3] * lax.axis_size("dom")
    scale = 1.0 / total_cells
    flattened = current.reshape(local_bands, -1)
    panel_flat = owned_panel.reshape(local_bands, -1)
    extended = extended_2(current, (("dom", 1),), 2)
    applied = hamiltonian_apply(extended, potential)
    ham_rows = jnp.einsum(
        "pc,bc->pb", panel_flat, applied.reshape(local_bands, -1), precision=lax.Precision.HIGHEST
    )
    over_rows = jnp.einsum("pc,bc->pb", panel_flat, flattened, precision=lax.Precision.HIGHEST)
    intersection, hamiltonian = lax.psum((over_rows * scale, ham_rows * scale), "dom")
    return (current, intersection, hamiltonian)


def solution(mesh):
    placed = (P("band", "dom", None, None), P("dom", None, None), P())
    return jax.shard_map(
        body,
        mesh=mesh,
        in_specs=placed,
        out_specs=(P("band", "dom", None, None), P(None, "band"), P(None, "band")),
        check_vma=False,
    )
```

profile of v0, /device:TPU:0, one launch (start us, length us, event | category | flops | bytes accessed | tf_op | source)
XLA Modules:
  0.0 314.2 jit_solution(11371170364938100870)
XLA Ops:
  7.2 0.0 all-reduce.3.cloned.1.call-start
  7.2 1.3 fusion.122
  8.5 0.0 copy-start
  8.5 1.0 copy.37
  9.5 6.8 %collective-permute-start.1 = (f32[64,2,8,128]{3,0,2,1:T(8,128)}, f32[64,2,8,128]{3,0,2,1:T(8,128)}, u32[]{:S(2)}, u32[]{:S(2)}) collective-permute-start(f32[64,2,8,128]{3,0,2,1:T(8,128)} %copy.37), channel_id=1, source_target_pairs={{1,0},{2,1},{3,2},{4,3},{5,4},{6,5},{7,6},{8,7},{9,8},{10,9},{11,1... | collective-permute-start | bytes 1572872 | tf_op jit(solution)/shard_map/ppermute | solution.py:19
  16.3 1.0 copy.38
  17.3 0.2 fusion.125
  17.4 1.0 fusion.123
  18.4 1.3 fusion.126
  19.7 1.3 fusion.127
  21.0 1.7 fusion.128
  22.8 1.6 fusion.124
  24.3 1.7 fusion.129
  26.0 1.7 fusion.130
  28.5 0.7 copy.45
  29.1 1.0 copy.40
  30.1 1.7 copy.41
  31.8 1.5 copy.43
  33.3 1.5 copy.46
  34.8 0.6 copy.48
  35.4 0.6 copy.49
  36.1 0.6 copy-done.13
  36.6 1.6 copy.47
  38.2 1.6 copy.50
  39.8 1.4 copy.39
  41.3 1.3 copy.42
  42.6 1.6 copy.52
  44.2 1.6 copy.53
  45.8 1.6 copy.51
  47.4 1.6 copy.54
  49.0 1.2 constant_dynamic-update-slice_fusion.1
  50.2 0.6 constant_dynamic-update-slice_fusion
  50.8 1.4 constant_dynamic-update-slice_fusion.2
  52.3 0.3 copy-done.4
  52.5 4.1 %broadcast_multiply_fusion = (f32[64,4,8,128]{3,0,2,1:T(8,128)S(1)}, f32[64,4,8,128]{3,0,2,1:T(8,128)S(1)}) fusion(f32[4,8,128]{2,1,0:T(8,128)} %param.4, f32[64,4,8,1]{3,0,2,1:T(8,128)S(1)} %copy-done.4, f32[64,4,8,127]{3,0,2,1:T(8,128)} %copy.54, f32[64,4,8,127]{3,0,2,1:T(8,128)S(1)} %copy-done.5, f32[64,4,8,1]{3,0,2,1:T(8,128)S(1)} %copy-done.3, ...), kind=kLoop, calls=%fused_computation.115 | loop fusion | flops 9175040 | bytes 15745024 | tf_op jit(solution)/shard_map/div | solution.py:47
  56.7 0.1 fusion.113
  56.8 0.2 fusion.115
  57.0 0.2 fusion.117
  57.2 0.4 fusion.118
  57.6 0.4 fusion.120
  58.0 0.4 fusion.119
  58.4 0.1 collective-permute-start.2
  58.4 5.7 %collective-permute-start.3 = (f32[64,2,8,128]{3,0,2,1:T(8,128)S(1)}, f32[64,2,8,128]{3,0,2,1:T(8,128)S(1)}, u32[]{:S(2)}, u32[]{:S(2)}) collective-permute-start(f32[64,2,8,128]{3,0,2,1:T(8,128)S(1)} %get-tuple-element.31), channel_id=1, source_target_pairs={{1,0},{2,1},{3,2},{4,3},{5,4},{6,5},{7,6},{8,7},{9,8},{10,9},{11,1... | collective-permute-start | bytes 1572872 | tf_op jit(solution)/shard_map/ppermute | solution.py:19
  64.2 0.4 fusion.121
  64.6 16.3 %collective-permute-done.2 = f32[64,2,8,128]{3,0,2,1:T(8,128)S(1)} collective-permute-done((f32[64,2,8,128]{3,0,2,1:T(8,128)S(1)}, f32[64,2,8,128]{3,0,2,1:T(8,128)S(1)}, u32[]{:S(2)}, u32[]{:S(2)}) %collective-permute-start.2) | collective-permute-done | bytes 524320 | tf_op jit(solution)/shard_map/ppermute | solution.py:16
  80.8 3.8 %collective-permute-done.3 = f32[64,2,8,128]{3,0,2,1:T(8,128)S(1)} collective-permute-done((f32[64,2,8,128]{3,0,2,1:T(8,128)S(1)}, f32[64,2,8,128]{3,0,2,1:T(8,128)S(1)}, u32[]{:S(2)}, u32[]{:S(2)}) %collective-permute-start.3) | collective-permute-done | bytes 524320 | tf_op jit(solution)/shard_map/ppermute | solution.py:19
  84.6 3.6 %broadcast_select_fusion = (f32[64,4,8,128]{3,0,2,1:T(8,128)}, f32[64,4,8,128]{3,0,2,1:T(8,128)S(1)}) fusion(pred[]{:T(512)S(6)} %eq.3, f32[64,4,8,128]{3,2,1,0:T(8,128)S(1)} %copy-done, f32[64,4,8,128]{3,0,2,1:T(8,128)S(1)} %get-tuple-element.11, f32[4,8,128]{2,1,0:T(8,128)S(1)} %broadcast_multiply_fusion.1, f32[64,4,8,1]{3,0,2,1:T(8,128)S(1)} %get-tuple-element.45, ...), kind=kLoop, calls=%fused_computation.114 | loop fusion | flops 10747904 | bytes 14696449 | tf_op jit(solution)/shard_map/jit(_where)/select_n | solution.py:26
  88.2 1.1 fusion.112
  89.3 1.4 fusion.108
  90.7 1.3 fusion.106
  92.1 1.7 fusion.105
  93.8 1.7 fusion.107
  95.4 0.0 all-reduce.3.cloned.1.call-update
  95.5 0.3 collective-permute-start.4
  95.7 5.5 %collective-permute-start.5 = (f32[64,2,8,128]{3,0,2,1:T(8,128)}, f32[64,2,8,128]{3,0,2,1:T(8,128)}, u32[]{:S(2)}, u32[]{:S(2)}) collective-permute-start(f32[64,2,8,128]{3,0,2,1:T(8,128)} %get-tuple-element.29), channel_id=1, source_target_pairs={{1,0},{2,1},{3,2},{4,3},{5,4},{6,5},{7,6},{8,7},{9,8},{10,9},{11,1... | collective-permute-start | bytes 1572872 | tf_op jit(solution)/shard_map/ppermute | solution.py:19
  101.2 1.4 fusion.110
  102.6 1.7 fusion.104
  104.3 0.7 fusion.109
  105.0 1.6 copy.30
  106.6 0.7 fusion.111
  107.3 113.6 %all-reduce.3.cloned.1.call-done = f32[64,4,8,128]{3,0,2,1:T(8,128)} async-done(((f32[64,4,8,128]{3,0,2,1:T(8,128)}), f32[64,4,8,128]{3,0,2,1:T(8,128)}) %all-reduce.3.cloned.1.call-update) | async-done | bytes 1048592 | tf_op jit(solution)/shard_map/psum | solution.py:26
  220.9 2.3 fusion.1
  223.2 6.2 %fusion = f32[64,64]{1,0:T(8,128)S(1)} fusion(f32[64,4,8,128]{3,0,2,1:T(8,128)S(1)} %copy-done.16, f32[64,4,8,128]{3,0,2,1:T(8,128)S(1)} %get-tuple-element.9, f32[64,2,8,128]{3,0,2,1:T(8,128)} %collective-permute-done.5, f32[64,2,8,128]{3,0,2,1:T(8,128)} %collective-permute-done.4, f32[64,4,6,128]{3,0,2,1:T(8,128)} %get-tuple-element.25, ...), kind=kOutput, calls=%fused_computation.9 | convolution fusion | flops 210767872 | bytes 11567104 | tf_op jit(solution)/shard_map/pc,bc->pb/dot_general | solution.py:67
  229.5 77.9 %all-reduce = (f32[64,64]{1,0:T(8,128)}, f32[64,64]{1,0:T(8,128)}) all-reduce(f32[64,64]{1,0:T(8,128)S(1)} %fusion.1, f32[64,64]{1,0:T(8,128)S(1)} %fusion), channel_id=1, replica_groups=mesh['band'=16,'dom'=16] {'dom'}, use_global_device_ids=true, to_apply=%region_1.2 | all-reduce | flops 8192 | bytes 65536 | tf_op jit(solution)/shard_map/psum | solution.py:71
  (46 shorter events, 0.2 us)
Async XLA Ops:
  7.2 213.7 %all-reduce.3.cloned.1.call-start = ((), (), s32[]{:S(2)}) async-start(), calls=%async_computation | async-start | bytes 2097152 | tf_op jit(solution)/shard_map/psum | solution.py:26
  8.5 8.8 %copy-start = (f32[64,4,8,128]{3,2,1,0:T(8,128)S(1)}, f32[64,4,8,128]{3,2,1,0:T(8,128)}, u32[]{:S(2)}) copy-start(f32[64,4,8,128]{3,2,1,0:T(8,128)} %param.3) | copy-start | bytes 3145732
  9.5 41.3 %collective-permute-start.1 = (f32[64,2,8,128]{3,0,2,1:T(8,128)}, f32[64,2,8,128]{3,0,2,1:T(8,128)}, u32[]{:S(2)}, u32[]{:S(2)}) collective-permute-start(f32[64,2,8,128]{3,0,2,1:T(8,128)} %copy.37), channel_id=1, source_target_pairs={{1,0},{2,1},{3,2},{4,3},{5,4},{6,5},{7,6},{8,7},{9,8},{10,9},{11,1... | collective-permute-start | bytes 1572872 | tf_op jit(solution)/shard_map/ppermute | solution.py:19
  17.3 31.7 %collective-permute-start = (f32[64,2,8,128]{3,0,2,1:T(8,128)}, f32[64,2,8,128]{3,0,2,1:T(8,128)}, u32[]{:S(2)}, u32[]{:S(2)}) collective-permute-start(f32[64,2,8,128]{3,0,2,1:T(8,128)} %copy.38), channel_id=1, source_target_pairs={{0,1},{1,2},{2,3},{3,4},{4,5},{5,6},{6,7},{7,8},{8,9},{9,10},{10,1... | collective-permute-start | bytes 1572872 | tf_op jit(solution)/shard_map/ppermute | solution.py:16
  26.0 1.7 copy-start.18
  27.7 4.2 %copy-start.15 = (f32[64,4,7,128]{3,2,1,0:T(8,128)S(1)}, f32[64,4,7,128]{3,2,1,0:T(8,128)}, u32[]{:S(2)}) copy-start(f32[64,4,7,128]{3,2,1,0:T(8,128)} %get-tuple-element.58) | copy-start | bytes 2752516
  33.3 2.1 copy-start.14
  35.4 1.2 copy-start.13
  36.0 2.2 copy-start.12
  38.2 1.6 copy-start.7
  38.2 3.0 copy-start.6
  39.8 2.8 copy-start.11
  41.3 2.9 copy-start.10
  44.2 1.6 copy-start.9
  45.8 1.6 copy-start.8
  49.0 3.3 %copy-start.5 = (f32[64,4,8,127]{3,0,2,1:T(8,128)S(1)}, f32[64,4,8,127]{3,0,2,1:T(8,128)}, u32[]{:S(2)}) copy-start(f32[64,4,8,127]{3,0,2,1:T(8,128)} %copy.51) | copy-start | bytes 3121156
  50.1 2.1 copy-start.1
  50.1 2.1 copy-start.2
  50.2 2.1 copy-start.3
  50.2 2.3 copy-start.4
  58.4 22.5 %collective-permute-start.2 = (f32[64,2,8,128]{3,0,2,1:T(8,128)S(1)}, f32[64,2,8,128]{3,0,2,1:T(8,128)S(1)}, u32[]{:S(2)}, u32[]{:S(2)}) collective-permute-start(f32[64,2,8,128]{3,0,2,1:T(8,128)S(1)} %get-tuple-element.30), channel_id=1, source_target_pairs={{0,1},{1,2},{2,3},{3,4},{4,5},{5,6},{6,7},{7,8},{8,9},{9,10},{10,1... | collective-permute-start | bytes 1572872 | tf_op jit(solution)/shard_map/ppermute | solution.py:16
  58.4 26.2 %collective-permute-start.3 = (f32[64,2,8,128]{3,0,2,1:T(8,128)S(1)}, f32[64,2,8,128]{3,0,2,1:T(8,128)S(1)}, u32[]{:S(2)}, u32[]{:S(2)}) collective-permute-start(f32[64,2,8,128]{3,0,2,1:T(8,128)S(1)} %get-tuple-element.31), channel_id=1, source_target_pairs={{1,0},{2,1},{3,2},{4,3},{5,4},{6,5},{7,6},{8,7},{9,8},{10,9},{11,1... | collective-permute-start | bytes 1572872 | tf_op jit(solution)/shard_map/ppermute | solution.py:19
  95.5 127.7 %collective-permute-start.4 = (f32[64,2,8,128]{3,0,2,1:T(8,128)}, f32[64,2,8,128]{3,0,2,1:T(8,128)}, u32[]{:S(2)}, u32[]{:S(2)}) collective-permute-start(f32[64,2,8,128]{3,0,2,1:T(8,128)} %get-tuple-element.28), channel_id=1, source_target_pairs={{0,1},{1,2},{2,3},{3,4},{4,5},{5,6},{6,7},{7,8},{8,9},{9,10},{10,1... | collective-permute-start | bytes 1572872 | tf_op jit(solution)/shard_map/ppermute | solution.py:16
  95.7 127.5 %collective-permute-start.5 = (f32[64,2,8,128]{3,0,2,1:T(8,128)}, f32[64,2,8,128]{3,0,2,1:T(8,128)}, u32[]{:S(2)}, u32[]{:S(2)}) collective-permute-start(f32[64,2,8,128]{3,0,2,1:T(8,128)} %get-tuple-element.29), channel_id=1, source_target_pairs={{1,0},{2,1},{3,2},{4,3},{5,4},{6,5},{7,6},{8,7},{9,8},{10,9},{11,1... | collective-permute-start | bytes 1572872 | tf_op jit(solution)/shard_map/ppermute | solution.py:19
  106.6 116.7 %copy-start.19 = (f32[4,8,128]{2,1,0:T(8,128)S(1)}, f32[4,8,128]{2,1,0:T(8,128)}, u32[]{:S(2)}) copy-start(f32[4,8,128]{2,1,0:T(8,128)} %param.4) | copy-start | bytes 49156
  220.9 2.3 copy-start.16
  220.9 2.4 copy-start.17
Sparse Core Ops, SparseCore 0:
  95.6 125.2 all-reduce.2
where the time goes:
time: 315 us; the launch traced here: 314 us
  waiting for transfers between devices  134 us (43%)
  blocking collectives  77.9 us (25%)
  local copies, waits for them, and re-layouts  53 us (17%)
  starting transfers between devices  18.3 us (6%)
  between operations  15.1 us (5%)
  matrix products  8.52 us (3%)
  other arithmetic  7.73 us (2%)
    psum x1, waiting for transfers between devices, broadcast(): return lax.psum(jnp.where(mine, array, jnp.zeros_like(array)), axis)  114 us
    psum x1, blocking collectives, body(): lax.psum((over_rows * scale, ham_rows * scale), 'dom')  77.9 us
    unnamed x60, local copies, waits for them, and re-layouts  25.5 us
    ppermute x3, starting transfers between devices, extended_2(): lax.ppermute(lax.slice_in_dim(block, 0, width, axis=dim), axis, backward)  18 us
    ppermute x3, waiting for transfers between devices, extended_2(): lax.ppermute(lax.slice_in_dim(block, block.shape[dim] - width, None, axis...  16.3 us
    slice x8, local copies, waits for them, and re-layouts, lap_periodic(): jnp.roll(grid_field, 2, which_axis) + jnp.roll(grid_field, -2, which_axis)  6.59 us
  transfers between devices with their start and end apart: 7, of which 3 were waited for; matrix products, arithmetic and copies ran while one was open for 13% of the time, Pallas kernels for 0%

commit v1 on v0

--- a/solution.py
+++ b/solution.py
@@ -5,6 +5,7 @@
 
 center = 4.9
 halfwidth = 4.1
+_work_sector = lambda packet, device_axis: jax.lax.all_gather(packet, device_axis).sum(axis=0)
 
 
 def extended_2(block, sides, width):
@@ -23,7 +24,7 @@
 
 def broadcast(array, axis, root):
     mine = lax.axis_index(axis) == root
-    return lax.psum(jnp.where(mine, array, jnp.zeros_like(array)), axis)
+    return _work_sector(jnp.where(mine, array, jnp.zeros_like(array)), axis)
 
 
 def lap_periodic(grid_field, which_axis):

time: 315 us -> 281 us (0.89)
  local copies, waits for them, and re-layouts: 53 us -> 18.8 us
  waiting for transfers between devices: 134 us -> 120 us
  other arithmetic: 7.73 us -> 18.5 us
  blocking collectives: 77.9 us -> 82.2 us
  matrix products: 8.52 us -> 4.28 us
    psum x1 -> x0, waiting for transfers between devices: 114 us -> none  [broadcast(): return lax.psum(jnp.where(mine, array, jnp.zeros_like(array)), axis)]
    all_gather x0 -> x1, waiting for transfers between devices: none -> 63.4 us  [jax.lax.all_gather(packet, device_axis).sum(axis=0)]
    ppermute x3, waiting for transfers between devices: 16.3 us -> 43.1 us  [extended_2(): lax.ppermute(lax.slice_in_dim(block, block.shape[dim] - width, None, axis...]
    unnamed x60 -> x17, local copies, waits for them, and re-layouts: 25.5 us -> 0.07 us
    ppermute x3, waiting for transfers between devices: 3.82 us -> 13.4 us  [extended_2(): lax.ppermute(lax.slice_in_dim(block, 0, width, axis=dim), axis, backward)]
    reduce_sum x0 -> x1, other arithmetic: none -> 7.91 us  [jax.lax.all_gather(packet, device_axis).sum(axis=0)]
    slice x4, local copies, waits for them, and re-layouts: 5.53 us -> 1.15 us  [lap_periodic(): jnp.roll(grid_field, -1, which_axis)]
    psum x1, blocking collectives: 77.9 us -> 82.2 us  [body(): lax.psum((over_rows * scale, ham_rows * scale), 'dom')]
  transfers between devices with their start and end apart: 7 -> 7, of which waited for: 3 -> 7; matrix products, arithmetic and copies ran while one was open for 13% -> 6% of each run, Pallas kernels for 0% -> 0%
where the time goes in v1:
time: 281 us; the launch traced here: 280 us
  waiting for transfers between devices  120 us (43%)
  blocking collectives  82.2 us (29%)
  starting transfers between devices  20.9 us (7%)
  local copies, waits for them, and re-layouts  18.8 us (7%)
  other arithmetic  18.5 us (7%)
  between operations  15 us (5%)
  matrix products  4.28 us (2%)
    psum x1, blocking collectives, body(): lax.psum((over_rows * scale, ham_rows * scale), 'dom')  82.2 us
    all_gather x1, waiting for transfers between devices, jax.lax.all_gather(packet, device_axis).sum(axis=0)  63.4 us
    ppermute x3, waiting for transfers between devices, extended_2(): lax.ppermute(lax.slice_in_dim(block, block.shape[dim] - width, None, axis...  43.1 us
    ppermute x3, starting transfers between devices, extended_2(): lax.ppermute(lax.slice_in_dim(block, 0, width, axis=dim), axis, backward)  16.2 us
    ppermute x3, waiting for transfers between devices, extended_2(): lax.ppermute(lax.slice_in_dim(block, 0, width, axis=dim), axis, backward)  13.4 us
    reduce_sum x1, other arithmetic, jax.lax.all_gather(packet, device_axis).sum(axis=0)  7.91 us
    slice x8, local copies, waits for them, and re-layouts, lap_periodic(): jnp.roll(grid_field, 1, which_axis) + jnp.roll(grid_field, -1, which_axis)  7.03 us
    slice x8, local copies, waits for them, and re-layouts, lap_periodic(): jnp.roll(grid_field, 2, which_axis) + jnp.roll(grid_field, -2, which_axis)  6.73 us
  transfers between devices with their start and end apart: 7, of which 7 were waited for; matrix products, arithmetic and copies ran while one was open for 6% of the time, Pallas kernels for 0%

profile of v1, /device:TPU:0, one launch (start us, length us, event | category | flops | bytes accessed | tf_op | source)
XLA Modules:
  0.0 279.5 jit_solution(364802518205164511)
XLA Ops:
  7.2 0.0 copy-start
  7.2 0.0 all-gather.3.cloned.1.call-start
  7.2 2.3 fusion.85
  9.6 1.5 collective-permute-start
  11.0 5.3 %collective-permute-start.1 = (f32[64,2,8,128]{3,2,1,0:T(8,128)}, f32[64,2,8,128]{3,2,1,0:T(8,128)S(1)}, u32[]{:S(2)}, u32[]{:S(2)}) collective-permute-start(f32[64,2,8,128]{3,2,1,0:T(8,128)} %get-tuple-element.48), channel_id=1, source_target_pairs={{1,0},{2,1},{3,2},{4,3},{5,4},{6,5},{7,6},{8,7},{9,8},{10,9},{11,1... | collective-permute-start | bytes 1572872 | tf_op jit(solution)/shard_map/ppermute | solution.py:20
  16.3 0.0 copy-done
  16.3 1.4 fusion.91
  17.7 1.7 fusion.90
  19.4 1.6 fusion.87
  21.1 1.7 fusion.93
  22.8 1.7 fusion.92
  24.5 1.7 fusion.89
  26.2 0.0 copy-start.7
  26.2 0.9 fusion.86
  27.0 0.8 fusion.88
  28.5 0.0 copy-done.7
  28.5 5.3 %collective-permute-done = f32[64,2,8,128]{3,2,1,0:T(8,128)S(1)} collective-permute-done((f32[64,2,8,128]{3,2,1,0:T(8,128)}, f32[64,2,8,128]{3,2,1,0:T(8,128)S(1)}, u32[]{:S(2)}, u32[]{:S(2)}) %collective-permute-start) | collective-permute-done | bytes 524320 | tf_op jit(solution)/shard_map/ppermute | solution.py:17
  33.8 0.0 copy-start.2
  33.8 0.0 copy-start.3
  33.8 0.0 copy-start.4
  33.8 0.0 copy-start.5
  33.9 0.1 constant_dynamic-update-slice_fusion
  34.0 3.4 %collective-permute-done.1 = f32[64,2,8,128]{3,2,1,0:T(8,128)S(1)} collective-permute-done((f32[64,2,8,128]{3,2,1,0:T(8,128)}, f32[64,2,8,128]{3,2,1,0:T(8,128)S(1)}, u32[]{:S(2)}, u32[]{:S(2)}) %collective-permute-start.1) | collective-permute-done | bytes 524320 | tf_op jit(solution)/shard_map/ppermute | solution.py:20
  37.4 0.0 copy-done.6
  37.4 0.0 copy-done.2
  37.4 0.0 copy-done.3
  37.4 0.0 copy-done.4
  37.5 0.0 copy-done.5
  37.5 4.6 %broadcast_multiply_fusion = (f32[64,4,8,128]{3,2,1,0:T(8,128)S(1)}, f32[64,4,8,128]{3,2,1,0:T(8,128)S(1)}) fusion(f32[64,4,8,128]{3,2,1,0:T(8,128)S(1)} %copy-done, f32[4,8,128]{2,1,0:T(8,128)S(1)} %copy-done.7, f32[64,4,8,1]{3,2,1,0:T(8,128)} %get-tuple-element.62, f32[64,4,8,127]{3,2,1,0:T(8,128)} %get-tuple-element.64, ...), kind=kLoop, calls=%fused_computation.95 | loop fusion | flops 9175040 | bytes 15745024 | tf_op jit(solution)/shard_map/div | solution.py:48
  42.1 0.2 fusion.77
  42.3 0.1 fusion.76
  42.3 0.2 fusion.80
  42.6 0.4 fusion.81
  43.0 0.4 fusion.83
  43.3 0.3 fusion.78
  43.6 0.4 fusion.82
  44.0 2.7 collective-permute-start.2
  46.7 5.4 %collective-permute-start.3 = (f32[64,2,8,128]{3,2,1,0:T(8,128)S(1)}, f32[64,2,8,128]{3,2,1,0:T(8,128)S(1)}, u32[]{:S(2)}, u32[]{:S(2)}) collective-permute-start(f32[64,2,8,128]{3,2,1,0:T(8,128)S(1)} %get-tuple-element.28), channel_id=1, source_target_pairs={{1,0},{2,1},{3,2},{4,3},{5,4},{6,5},{7,6},{8,7},{9,8},{10,9},{11,1... | collective-permute-start | bytes 1572872 | tf_op jit(solution)/shard_map/ppermute | solution.py:20
  52.1 0.2 fusion.79
  52.3 0.4 fusion.84
  52.6 15.7 %collective-permute-done.2 = f32[64,2,8,128]{3,2,1,0:T(8,128)S(1)} collective-permute-done((f32[64,2,8,128]{3,2,1,0:T(8,128)S(1)}, f32[64,2,8,128]{3,2,1,0:T(8,128)S(1)}, u32[]{:S(2)}, u32[]{:S(2)}) %collective-permute-start.2) | collective-permute-done | bytes 524320 | tf_op jit(solution)/shard_map/ppermute | solution.py:17
  68.3 3.7 %collective-permute-done.3 = f32[64,2,8,128]{3,2,1,0:T(8,128)S(1)} collective-permute-done((f32[64,2,8,128]{3,2,1,0:T(8,128)S(1)}, f32[64,2,8,128]{3,2,1,0:T(8,128)S(1)}, u32[]{:S(2)}, u32[]{:S(2)}) %collective-permute-start.3) | collective-permute-done | bytes 524320 | tf_op jit(solution)/shard_map/ppermute | solution.py:20
  72.0 3.5 %broadcast_select_fusion = (f32[64,4,8,128]{3,2,1,0:T(8,128)}, f32[64,4,8,128]{3,2,1,0:T(8,128)S(1)}) fusion(pred[]{:T(512)S(6)} %eq.3, f32[64,4,8,128]{3,2,1,0:T(8,128)S(1)} %copy-done, f32[64,4,8,128]{3,2,1,0:T(8,128)S(1)} %get-tuple-element.8, f32[4,8,128]{2,1,0:T(8,128)S(1)} %broadcast_multiply_fusion.1, f32[64,4,8,1]{3,2,1,0:T(8,128)S(1)} %get-tuple-element.42, ...), kind=kLoop, calls=%fused_computation.94 | loop fusion | flops 10747904 | bytes 14696449 | tf_op jit(solution)/shard_map/jit(_where)/select_n | solution.py:27
  75.5 0.0 all-gather.3.cloned.1.call-update
  75.5 0.1 fusion.75
  75.6 0.4 collective-permute-start.4
  75.9 5.6 %collective-permute-start.5 = (f32[64,2,8,128]{3,2,1,0:T(8,128)S(1)}, f32[64,2,8,128]{3,2,1,0:T(8,128)S(1)}, u32[]{:S(2)}, u32[]{:S(2)}) collective-permute-start(f32[64,2,8,128]{3,2,1,0:T(8,128)S(1)} %get-tuple-element.26), channel_id=1, source_target_pairs={{1,0},{2,1},{3,2},{4,3},{5,4},{6,5},{7,6},{8,7},{9,8},{10,9},{11,1... | collective-permute-start | bytes 1572872 | tf_op jit(solution)/shard_map/ppermute | solution.py:20
  81.5 0.2 fusion.74
  81.6 0.4 fusion.69
  82.0 0.2 fusion.73
  82.3 0.3 fusion.71
  82.5 0.4 fusion.68
  82.9 0.4 fusion.70
  83.3 0.2 fusion.72
  83.4 0.4 fusion.67
  83.8 22.2 %collective-permute-done.4 = f32[64,2,8,128]{3,2,1,0:T(8,128)S(1)} collective-permute-done((f32[64,2,8,128]{3,2,1,0:T(8,128)S(1)}, f32[64,2,8,128]{3,2,1,0:T(8,128)S(1)}, u32[]{:S(2)}, u32[]{:S(2)}) %collective-permute-start.4) | collective-permute-done | bytes 524320 | tf_op jit(solution)/shard_map/ppermute | solution.py:17
  106.0 6.3 %collective-permute-done.5 = f32[64,2,8,128]{3,2,1,0:T(8,128)S(1)} collective-permute-done((f32[64,2,8,128]{3,2,1,0:T(8,128)S(1)}, f32[64,2,8,128]{3,2,1,0:T(8,128)S(1)}, u32[]{:S(2)}, u32[]{:S(2)}) %collective-permute-start.5) | collective-permute-done | bytes 524320 | tf_op jit(solution)/shard_map/ppermute | solution.py:20
  112.3 2.5 fusion.10
  114.9 63.4 %all-gather.3.cloned.1.call-done = f32[1024,4,8,128]{3,2,1,0:T(8,128)} async-done(((f32[64,4,8,128]{3,2,1,0:T(8,128)}), f32[1024,4,8,128]{3,2,1,0:T(8,128)}) %all-gather.3.cloned.1.call-update) | async-done | bytes 16777232 | tf_op jit(solution)/shard_map/all_gather | solution.py:8
  178.3 7.9 %reduce_sum.9 = f32[64,4,8,128]{3,2,1,0:T(8,128)S(1)} reduce(f32[16,64,4,8,128]{4,3,2,1,0:T(8,128)} %bitcast.15, f32[]{:T(128)} %constant.29.clone.1), dimensions={0}, to_apply=%region_0.1 | reduce | flops 3932160 | bytes 17825796 | tf_op jit(solution)/shard_map/reduce_sum | solution.py:8
  186.2 0.0 copy-done.1
  186.2 2.1 fusion.1
  188.3 2.1 fusion
  190.5 82.2 %all-reduce = (f32[64,64]{1,0:T(8,128)}, f32[64,64]{1,0:T(8,128)}) all-reduce(f32[64,64]{1,0:T(8,128)S(1)} %fusion.1, f32[64,64]{1,0:T(8,128)S(1)} %fusion), channel_id=1, replica_groups=mesh['band'=16,'dom'=16] {'dom'}, use_global_device_ids=true, to_apply=%region_1.2 | all-reduce | flops 8192 | bytes 65536 | tf_op jit(solution)/shard_map/psum | solution.py:72
  (5 shorter events, 0.1 us)
Async XLA Ops:
  7.2 9.2 %copy-start = (f32[64,4,8,128]{3,2,1,0:T(8,128)S(1)}, f32[64,4,8,128]{3,2,1,0:T(8,128)}, u32[]{:S(2)}) copy-start(f32[64,4,8,128]{3,2,1,0:T(8,128)} %param.3) | copy-start | bytes 3145732
  7.2 171.1 %all-gather.3.cloned.1.call-start = ((), (), s32[]{:S(2)}) async-start(), calls=%async_computation | async-start | bytes 17825792 | tf_op jit(solution)/shard_map/all_gather | solution.py:8
  9.6 24.2 %collective-permute-start = (f32[64,2,8,128]{3,2,1,0:T(8,128)}, f32[64,2,8,128]{3,2,1,0:T(8,128)S(1)}, u32[]{:S(2)}, u32[]{:S(2)}) collective-permute-start(f32[64,2,8,128]{3,2,1,0:T(8,128)} %get-tuple-element.47), channel_id=1, source_target_pairs={{0,1},{1,2},{2,3},{3,4},{4,5},{5,6},{6,7},{7,8},{8,9},{9,10},{10,1... | collective-permute-start | bytes 1572872 | tf_op jit(solution)/shard_map/ppermute | solution.py:17
  11.0 26.3 %collective-permute-start.1 = (f32[64,2,8,128]{3,2,1,0:T(8,128)}, f32[64,2,8,128]{3,2,1,0:T(8,128)S(1)}, u32[]{:S(2)}, u32[]{:S(2)}) collective-permute-start(f32[64,2,8,128]{3,2,1,0:T(8,128)} %get-tuple-element.48), channel_id=1, source_target_pairs={{1,0},{2,1},{3,2},{4,3},{5,4},{6,5},{7,6},{8,7},{9,8},{10,9},{11,1... | collective-permute-start | bytes 1572872 | tf_op jit(solution)/shard_map/ppermute | solution.py:20
  26.2 2.3 copy-start.7
  33.8 3.6 %copy-start.6 = (f32[64,4,6,128]{3,2,1,0:T(8,128)S(1)}, f32[64,4,6,128]{3,2,1,0:T(8,128)}, u32[]{:S(2)}) copy-start(f32[64,4,6,128]{3,2,1,0:T(8,128)} %get-tuple-element.52) | copy-start | bytes 2359300
  33.8 3.6 %copy-start.2 = (f32[64,4,8,126]{3,2,1,0:T(8,128)S(1)}, f32[64,4,8,126]{3,2,1,0:T(8,128)}, u32[]{:S(2)}) copy-start(f32[64,4,8,126]{3,2,1,0:T(8,128)} %get-tuple-element.60) | copy-start | bytes 3096580
  33.8 3.6 %copy-start.3 = (f32[64,4,8,2]{3,2,1,0:T(8,128)S(1)}, f32[64,4,8,2]{3,2,1,0:T(8,128)}, u32[]{:S(2)}) copy-start(f32[64,4,8,2]{3,2,1,0:T(8,128)} %get-tuple-element.57) | copy-start | bytes 49156
  33.8 3.6 %copy-start.4 = (f32[64,4,8,2]{3,2,1,0:T(8,128)S(1)}, f32[64,4,8,2]{3,2,1,0:T(8,128)}, u32[]{:S(2)}) copy-start(f32[64,4,8,2]{3,2,1,0:T(8,128)} %get-tuple-element.58) | copy-start | bytes 49156
  33.8 3.6 %copy-start.5 = (f32[64,4,6,128]{3,2,1,0:T(8,128)S(1)}, f32[64,4,6,128]{3,2,1,0:T(8,128)}, u32[]{:S(2)}) copy-start(f32[64,4,6,128]{3,2,1,0:T(8,128)} %get-tuple-element.51) | copy-start | bytes 2359300
  44.0 24.3 %collective-permute-start.2 = (f32[64,2,8,128]{3,2,1,0:T(8,128)S(1)}, f32[64,2,8,128]{3,2,1,0:T(8,128)S(1)}, u32[]{:S(2)}, u32[]{:S(2)}) collective-permute-start(f32[64,2,8,128]{3,2,1,0:T(8,128)S(1)} %get-tuple-element.27), channel_id=1, source_target_pairs={{0,1},{1,2},{2,3},{3,4},{4,5},{5,6},{6,7},{7,8},{8,9},{9,10},{10,1... | collective-permute-start | bytes 1572872 | tf_op jit(solution)/shard_map/ppermute | solution.py:17
  46.7 25.3 %collective-permute-start.3 = (f32[64,2,8,128]{3,2,1,0:T(8,128)S(1)}, f32[64,2,8,128]{3,2,1,0:T(8,128)S(1)}, u32[]{:S(2)}, u32[]{:S(2)}) collective-permute-start(f32[64,2,8,128]{3,2,1,0:T(8,128)S(1)} %get-tuple-element.28), channel_id=1, source_target_pairs={{1,0},{2,1},{3,2},{4,3},{5,4},{6,5},{7,6},{8,7},{9,8},{10,9},{11,1... | collective-permute-start | bytes 1572872 | tf_op jit(solution)/shard_map/ppermute | solution.py:20
  75.5 110.7 %copy-start.1 = (f32[64,4,8,128]{3,2,1,0:T(8,128)}, f32[64,4,8,128]{3,2,1,0:T(8,128)S(1)}, u32[]{:S(2)}) copy-start(f32[64,4,8,128]{3,2,1,0:T(8,128)S(1)} %get-tuple-element.6) | copy-start | bytes 3145732
  75.6 30.4 %collective-permute-start.4 = (f32[64,2,8,128]{3,2,1,0:T(8,128)S(1)}, f32[64,2,8,128]{3,2,1,0:T(8,128)S(1)}, u32[]{:S(2)}, u32[]{:S(2)}) collective-permute-start(f32[64,2,8,128]{3,2,1,0:T(8,128)S(1)} %get-tuple-element.25), channel_id=1, source_target_pairs={{0,1},{1,2},{2,3},{3,4},{4,5},{5,6},{6,7},{7,8},{8,9},{9,10},{10,1... | collective-permute-start | bytes 1572872 | tf_op jit(solution)/shard_map/ppermute | solution.py:17
  75.9 36.4 %collective-permute-start.5 = (f32[64,2,8,128]{3,2,1,0:T(8,128)S(1)}, f32[64,2,8,128]{3,2,1,0:T(8,128)S(1)}, u32[]{:S(2)}, u32[]{:S(2)}) collective-permute-start(f32[64,2,8,128]{3,2,1,0:T(8,128)S(1)} %get-tuple-element.26), channel_id=1, source_target_pairs={{1,0},{2,1},{3,2},{4,3},{5,4},{6,5},{7,6},{8,7},{9,8},{10,9},{11,1... | collective-permute-start | bytes 1572872 | tf_op jit(solution)/shard_map/ppermute | solution.py:20
Sparse Core Ops, SparseCore 0:
  75.6 102.6 all-gather.2
